TPU v7x, 32 devices: a whole 2x2x4 slice. The times are simulated.
32 devices in a mesh: grid: 8 (over z, x), mem: 4 (over y, core).
Axes of the slice: x: 2, y: 2, z: 4, core: 2. Of those that a mesh axis runs over, the one named last changes fastest.
Arguments:
- members: bfloat16 [80, 4, 16, 512], P('mem', None, 'grid'), may hold values from -0.8984375 to 0.8984375
- innovation: float32 [4, 16, 512], P(None, 'grid'), may hold values from -6 to 6
- observed_count: int32 [16, 512], P('grid'), may hold values from 0 to 3
- obs_precision: float32 [4], replicated, may hold values from 0.5 to 4
Outputs:
- recentred: bfloat16 [80, 4, 16, 512], P('mem', None, 'grid')
- increment: float32 [4, 16, 512], P('mem', 'grid')
All inputs are finite; a program needn't handle non-finite values.
Results may differ from a plain program's by a relative error of at most 0.0004.
Values may be sent and summed in bfloat16 or wider, within the bound.
No kernel may reach another device: no remote copies, remote signals or barrier semaphores. Data moves between devices by JAX's collectives and lax.ppermute only.
A program may use at most 64 MiB of HBM per device.

v0:
```python
import jax
import jax.numpy as jnp
from jax import lax
from jax.sharding import PartitionSpec as P

PASSES = 2
ITERS = 2
diffusion = 0.25


def padded(value, sides, width):
    for axis, dim in sides:
        devices, length = (lax.axis_size(axis), value.shape[dim])
        up = [(i, (i + 1) % devices) for i in range(devices - 1)]
        down = [(j, i) for i, j in up]
        last = lax.slice_in_dim(value, length - width, length, axis=dim)
        leading = lax.slice_in_dim(value, 0, width, axis=dim)
        before = lax.ppermute(last, axis, up)
        after = lax.ppermute(leading, axis, down)
        value = jnp.concatenate([before, value, after], axis=dim)
    return value


def smooth(field):
    for sweep_index in range(PASSES):
        extended = padded(field, (("grid", 2),), 1)
        centre = extended[:, :, 1:-1]
        field = centre + diffusion * (extended[:, :, :-2] + extended[:, :, 2:] - 2.0 * centre)
    for sweep_index in range(PASSES):
        field = field + diffusion * (jnp.roll(field, 1, 3) + jnp.roll(field, -1, 3) - 2.0 * field)
    return field


def member_total(product):
    summed = jnp.sum(product, axis=0)
    return summed


def norm_of(residual):
    return lax.psum(jnp.sum(residual * residual), ("grid", "mem"))


def local(members, innovation, observed_count, obs_precision):
    mem_index = lax.axis_index("mem")
    level_share = members.shape[1] // lax.axis_size("mem")
    perturbed = lax.all_to_all(members, "mem", split_axis=1, concat_axis=0, tiled=True)
    precision = lax.dynamic_slice_in_dim(obs_precision, mem_index * level_share, level_share, 0)
    local_innovation = lax.dynamic_slice_in_dim(innovation, mem_index * level_share, level_share, 0)
    weight = observed_count.astype(jnp.float32)[None] * precision[:, None, None]
    gradient = smooth(perturbed * (weight * local_innovation)[None])
    carried = jnp.zeros_like(gradient)
    residual = gradient
    direction = residual
    norm_now = norm_of(residual)
    for iteration in range(ITERS):
        smoothed = smooth(direction)
        total = member_total(perturbed * smoothed)
        back = smooth(perturbed * (weight * total)[None])
        image, smoothed = (direction + back, smoothed)
        step_size = norm_now / lax.psum(jnp.sum(direction * image), ("grid", "mem"))
        carried = carried + step_size * smoothed
        residual = residual - step_size * image
        if iteration + 1 < ITERS:
            norm_next = norm_of(residual)
            direction = residual + norm_next / norm_now * direction
            norm_now = norm_next
    increment = member_total(perturbed * carried)
    whole = lax.all_gather(increment, "mem", axis=0, tiled=True)
    recentred = (members.astype(jnp.float32) + whole[None]).astype(jnp.bfloat16)
    return (recentred, increment)


def solution(mesh):
    placed = (P("mem", None, "grid", None), P(None, "grid", None), P("grid", None), P())
    return jax.shard_map(
        local,
        mesh=mesh,
        in_specs=placed,
        out_specs=(P("mem", None, "grid", None), P("mem", "grid", None)),
        check_vma=False,
    )
```

profile of v0, /device:TPU:0, one launch (start us, length us, event | category | flops | bytes accessed | tf_op | source)
XLA Modules:
  0.0 294.0 jit_solution(12753605812569267372)
XLA Ops:
  0.6 1.7 copy.7
  2.3 4.3 %all-to-all-start = ((bf16[20,4,2,512]{3,2,0,1:T(2,128)(2,1)}), bf16[20,4,2,512]{3,2,0,1:T(2,128)(2,1)S(1)}, u32[]{:S(2)}, u32[]{:S(2)}) async-start(bf16[20,4,2,512]{3,2,0,1:T(2,128)(2,1)} %copy.7), calls=%async_computation | async-start | bytes 327680 | tf_op jit(solution)/shard_map/all_to_all | solution.py:46
  9.2 2.4 all-to-all-done
  12.0 3.9 %collective-permute-start = (f32[80,1,1,512]{3,2,0,1:T(1,128)S(1)}, f32[80,1,1,512]{3,2,0,1:T(1,128)S(1)}, u32[]{:S(2)}, u32[]{:S(2)}) collective-permute-start(f32[80,1,1,512]{3,2,0,1:T(1,128)S(1)} %get-tuple-element.69), channel_id=1, source_target_pairs={{0,4},{4,8},{8,12},{12,16},{16,20},{20,24},{24,28},{1,5},{5,9},{9,... | collective-permute-start | bytes 491528 | tf_op jit(solution)/shard_map/ppermute | solution.py:18
  17.2 1.7 collective-permute-done
  18.9 4.2 %collective-permute-done.1 = f32[80,1,1,512]{3,2,0,1:T(1,128)S(1)} collective-permute-done((f32[80,1,1,512]{3,2,0,1:T(1,128)S(1)}, f32[80,1,1,512]{3,2,0,1:T(1,128)S(1)}, u32[]{:S(2)}, u32[]{:S(2)}) %collective-permute-start.1) | collective-permute-done | bytes 163872 | tf_op jit(solution)/shard_map/ppermute | solution.py:19
  24.1 4.4 %collective-permute-start.2 = (f32[80,1,1,512]{3,2,0,1:T(1,128)S(1)}, f32[80,1,1,512]{3,2,0,1:T(1,128)S(1)}, u32[]{:S(2)}, u32[]{:S(2)}) collective-permute-start(f32[80,1,1,512]{3,2,0,1:T(1,128)S(1)} %get-tuple-element.67), channel_id=1, source_target_pairs={{0,4},{4,8},{8,12},{12,16},{16,20},{20,24},{24,28},{1,5},{5,9},{9,... | collective-permute-start | bytes 491528 | tf_op jit(solution)/shard_map/ppermute | solution.py:18
  29.8 1.5 collective-permute-done.2
  31.3 4.5 %collective-permute-done.3 = f32[80,1,1,512]{3,2,0,1:T(1,128)S(1)} collective-permute-done((f32[80,1,1,512]{3,2,0,1:T(1,128)S(1)}, f32[80,1,1,512]{3,2,0,1:T(1,128)S(1)}, u32[]{:S(2)}, u32[]{:S(2)}) %collective-permute-start.3) | collective-permute-done | bytes 163872 | tf_op jit(solution)/shard_map/ppermute | solution.py:19
  39.7 4.5 %collective-permute-start.4 = (f32[80,1,1,512]{3,2,0,1:T(1,128)S(1)}, f32[80,1,1,512]{3,2,0,1:T(1,128)S(1)}, u32[]{:S(2)}, u32[]{:S(2)}) collective-permute-start(f32[80,1,1,512]{3,2,0,1:T(1,128)S(1)} %get-tuple-element.57), channel_id=1, source_target_pairs={{0,4},{4,8},{8,12},{12,16},{16,20},{20,24},{24,28},{1,5},{5,9},{9,... | collective-permute-start | bytes 491528 | tf_op jit(solution)/shard_map/ppermute | solution.py:18
  45.5 1.5 collective-permute-done.4
  47.1 4.9 %collective-permute-done.5 = f32[80,1,1,512]{3,2,0,1:T(1,128)S(1)} collective-permute-done((f32[80,1,1,512]{3,2,0,1:T(1,128)S(1)}, f32[80,1,1,512]{3,2,0,1:T(1,128)S(1)}, u32[]{:S(2)}, u32[]{:S(2)}) %collective-permute-start.5) | collective-permute-done | bytes 163872 | tf_op jit(solution)/shard_map/ppermute | solution.py:19
  53.0 4.5 %collective-permute-start.6 = (f32[80,1,1,512]{3,2,0,1:T(1,128)S(1)}, f32[80,1,1,512]{3,2,0,1:T(1,128)S(1)}, u32[]{:S(2)}, u32[]{:S(2)}) collective-permute-start(f32[80,1,1,512]{3,2,0,1:T(1,128)S(1)} %get-tuple-element.55), channel_id=1, source_target_pairs={{0,4},{4,8},{8,12},{12,16},{16,20},{20,24},{24,28},{1,5},{5,9},{9,... | collective-permute-start | bytes 491528 | tf_op jit(solution)/shard_map/ppermute | solution.py:18
  58.8 1.5 collective-permute-done.6
  60.3 5.1 %collective-permute-done.7 = f32[80,1,1,512]{3,2,0,1:T(1,128)S(1)} collective-permute-done((f32[80,1,1,512]{3,2,0,1:T(1,128)S(1)}, f32[80,1,1,512]{3,2,0,1:T(1,128)S(1)}, u32[]{:S(2)}, u32[]{:S(2)}) %collective-permute-start.7) | collective-permute-done | bytes 163872 | tf_op jit(solution)/shard_map/ppermute | solution.py:19
  70.1 4.5 %collective-permute-start.8 = (f32[80,1,1,512]{3,2,0,1:T(1,128)S(1)}, f32[80,1,1,512]{3,2,0,1:T(1,128)S(1)}, u32[]{:S(2)}, u32[]{:S(2)}) collective-permute-start(f32[80,1,1,512]{3,2,0,1:T(1,128)S(1)} %get-tuple-element.45), channel_id=1, source_target_pairs={{0,4},{4,8},{8,12},{12,16},{16,20},{20,24},{24,28},{1,5},{5,9},{9,... | collective-permute-start | bytes 491528 | tf_op jit(solution)/shard_map/ppermute | solution.py:18
  77.5 5.1 %collective-permute-done.9 = f32[80,1,1,512]{3,2,0,1:T(1,128)S(1)} collective-permute-done((f32[80,1,1,512]{3,2,0,1:T(1,128)S(1)}, f32[80,1,1,512]{3,2,0,1:T(1,128)S(1)}, u32[]{:S(2)}, u32[]{:S(2)}) %collective-permute-start.9) | collective-permute-done | bytes 163872 | tf_op jit(solution)/shard_map/ppermute | solution.py:19
  83.5 4.5 %collective-permute-start.10 = (f32[80,1,1,512]{3,2,0,1:T(1,128)S(1)}, f32[80,1,1,512]{3,2,0,1:T(1,128)S(1)}, u32[]{:S(2)}, u32[]{:S(2)}) collective-permute-start(f32[80,1,1,512]{3,2,0,1:T(1,128)S(1)} %get-tuple-element.43), channel_id=1, source_target_pairs={{0,4},{4,8},{8,12},{12,16},{16,20},{20,24},{24,28},{1,5},{5,9},{9,... | collective-permute-start | bytes 491528 | tf_op jit(solution)/shard_map/ppermute | solution.py:18
  90.9 5.1 %collective-permute-done.11 = f32[80,1,1,512]{3,2,0,1:T(1,128)S(1)} collective-permute-done((f32[80,1,1,512]{3,2,0,1:T(1,128)S(1)}, f32[80,1,1,512]{3,2,0,1:T(1,128)S(1)}, u32[]{:S(2)}, u32[]{:S(2)}) %collective-permute-start.11) | collective-permute-done | bytes 163872 | tf_op jit(solution)/shard_map/ppermute | solution.py:19
  100.5 41.8 %all-reduce = (f32[]{:T(128)}, f32[]{:T(128)}) all-reduce(f32[]{:T(128)} %get-tuple-element.3, f32[]{:T(128)} %get-tuple-element.2), channel_id=1, replica_groups=mesh['grid'=8,'mem'=4] {'grid','mem'}, use_global_device_ids=true, to_apply=%region_1.2 | all-reduce | flops 2 | bytes 16 | tf_op jit(solution)/shard_map/psum | solution.py:40
  144.6 40.8 %psum.30 = f32[]{:T(128)} all-reduce(f32[]{:T(128)} %multiply_reduce_fusion.2), channel_id=1, replica_groups=mesh['grid'=8,'mem'=4] {'grid','mem'}, use_global_device_ids=true, to_apply=%region_6.7 | all-reduce | flops 1 | bytes 8 | tf_op jit(solution)/shard_map/psum | solution.py:40
  187.2 4.2 %collective-permute-start.12 = (f32[80,1,1,512]{3,2,0,1:T(1,128)S(1)}, f32[80,1,1,512]{3,2,0,1:T(1,128)S(1)}, u32[]{:S(2)}, u32[]{:S(2)}) collective-permute-start(f32[80,1,1,512]{3,2,0,1:T(1,128)S(1)} %get-tuple-element.33), channel_id=1, source_target_pairs={{0,4},{4,8},{8,12},{12,16},{16,20},{20,24},{24,28},{1,5},{5,9},{9,... | collective-permute-start | bytes 491528 | tf_op jit(solution)/shard_map/ppermute | solution.py:18
  192.7 5.1 %collective-permute-done.12 = f32[80,1,1,512]{3,2,0,1:T(1,128)S(1)} collective-permute-done((f32[80,1,1,512]{3,2,0,1:T(1,128)S(1)}, f32[80,1,1,512]{3,2,0,1:T(1,128)S(1)}, u32[]{:S(2)}, u32[]{:S(2)}) %collective-permute-start.12) | collective-permute-done | bytes 163872 | tf_op jit(solution)/shard_map/ppermute | solution.py:18
  199.6 3.5 %collective-permute-start.14 = (f32[80,1,1,512]{3,2,0,1:T(1,128)S(1)}, f32[80,1,1,512]{3,2,0,1:T(1,128)S(1)}, u32[]{:S(2)}, u32[]{:S(2)}) collective-permute-start(f32[80,1,1,512]{3,2,0,1:T(1,128)S(1)} %get-tuple-element.31), channel_id=1, source_target_pairs={{0,4},{4,8},{8,12},{12,16},{16,20},{20,24},{24,28},{1,5},{5,9},{9,... | collective-permute-start | bytes 491528 | tf_op jit(solution)/shard_map/ppermute | solution.py:18
  203.1 1.5 collective-permute-start.15
  206.0 4.4 %collective-permute-done.15 = f32[80,1,1,512]{3,2,0,1:T(1,128)S(1)} collective-permute-done((f32[80,1,1,512]{3,2,0,1:T(1,128)S(1)}, f32[80,1,1,512]{3,2,0,1:T(1,128)S(1)}, u32[]{:S(2)}, u32[]{:S(2)}) %collective-permute-start.15) | collective-permute-done | bytes 163872 | tf_op jit(solution)/shard_map/ppermute | solution.py:19
  215.0 3.7 %collective-permute-start.16 = (f32[80,1,1,512]{3,2,0,1:T(1,128)S(1)}, f32[80,1,1,512]{3,2,0,1:T(1,128)S(1)}, u32[]{:S(2)}, u32[]{:S(2)}) collective-permute-start(f32[80,1,1,512]{3,2,0,1:T(1,128)S(1)} %get-tuple-element.21), channel_id=1, source_target_pairs={{0,4},{4,8},{8,12},{12,16},{16,20},{20,24},{24,28},{1,5},{5,9},{9,... | collective-permute-start | bytes 491528 | tf_op jit(solution)/shard_map/ppermute | solution.py:18
  221.6 4.4 %collective-permute-done.17 = f32[80,1,1,512]{3,2,0,1:T(1,128)S(1)} collective-permute-done((f32[80,1,1,512]{3,2,0,1:T(1,128)S(1)}, f32[80,1,1,512]{3,2,0,1:T(1,128)S(1)}, u32[]{:S(2)}, u32[]{:S(2)}) %collective-permute-start.17) | collective-permute-done | bytes 163872 | tf_op jit(solution)/shard_map/ppermute | solution.py:19
  227.0 4.4 %collective-permute-start.18 = (f32[80,1,1,512]{3,2,0,1:T(1,128)S(1)}, f32[80,1,1,512]{3,2,0,1:T(1,128)S(1)}, u32[]{:S(2)}, u32[]{:S(2)}) collective-permute-start(f32[80,1,1,512]{3,2,0,1:T(1,128)S(1)} %get-tuple-element.19), channel_id=1, source_target_pairs={{0,4},{4,8},{8,12},{12,16},{16,20},{20,24},{24,28},{1,5},{5,9},{9,... | collective-permute-start | bytes 491528 | tf_op jit(solution)/shard_map/ppermute | solution.py:18
  234.2 5.1 %collective-permute-done.19 = f32[80,1,1,512]{3,2,0,1:T(1,128)S(1)} collective-permute-done((f32[80,1,1,512]{3,2,0,1:T(1,128)S(1)}, f32[80,1,1,512]{3,2,0,1:T(1,128)S(1)}, u32[]{:S(2)}, u32[]{:S(2)}) %collective-permute-start.19) | collective-permute-done | bytes 163872 | tf_op jit(solution)/shard_map/ppermute | solution.py:19
  243.6 42.2 %psum.31 = f32[]{:T(128)} all-reduce(f32[]{:T(128)} %fusion), channel_id=1, replica_groups=mesh['grid'=8,'mem'=4] {'grid','mem'}, use_global_device_ids=true, to_apply=%region_9.10 | all-reduce | flops 1 | bytes 8 | tf_op jit(solution)/shard_map/psum | solution.py:60
  287.4 5.7 %all-gather.1 = f32[4,2,512]{2,1,0:T(2,128)S(1)} all-gather(f32[1,2,512]{2,1,0:T(2,128)S(1)} %bitcast.46), channel_id=2, replica_groups=mesh['grid'=8,'mem'=4] {'mem'}, dimensions={0}, use_global_device_ids=true | all-gather | bytes 20480 | tf_op jit(solution)/shard_map/all_gather | solution.py:68
  (88 shorter events, 52.2 us)
Async XLA Ops:
  2.3 9.2 %all-to-all-start = ((bf16[20,4,2,512]{3,2,0,1:T(2,128)(2,1)}), bf16[20,4,2,512]{3,2,0,1:T(2,128)(2,1)S(1)}, u32[]{:S(2)}, u32[]{:S(2)}) async-start(bf16[20,4,2,512]{3,2,0,1:T(2,128)(2,1)} %copy.7), calls=%async_computation | async-start | bytes 327680 | tf_op jit(solution)/shard_map/all_to_all | solution.py:46
  6.6 0.7 copy-start.3
  6.6 1.2 copy-start.1
  12.0 6.9 %collective-permute-start = (f32[80,1,1,512]{3,2,0,1:T(1,128)S(1)}, f32[80,1,1,512]{3,2,0,1:T(1,128)S(1)}, u32[]{:S(2)}, u32[]{:S(2)}) collective-permute-start(f32[80,1,1,512]{3,2,0,1:T(1,128)S(1)} %get-tuple-element.69), channel_id=1, source_target_pairs={{0,4},{4,8},{8,12},{12,16},{16,20},{20,24},{24,28},{1,5},{5,9},{9,... | collective-permute-start | bytes 491528 | tf_op jit(solution)/shard_map/ppermute | solution.py:18
  15.9 7.2 %collective-permute-start.1 = (f32[80,1,1,512]{3,2,0,1:T(1,128)S(1)}, f32[80,1,1,512]{3,2,0,1:T(1,128)S(1)}, u32[]{:S(2)}, u32[]{:S(2)}) collective-permute-start(f32[80,1,1,512]{3,2,0,1:T(1,128)S(1)} %get-tuple-element.70), channel_id=1, source_target_pairs={{4,0},{8,4},{12,8},{16,12},{20,16},{24,20},{28,24},{5,1},{9,5},{13... | collective-permute-start | bytes 491528 | tf_op jit(solution)/shard_map/ppermute | solution.py:19
  24.1 7.2 %collective-permute-start.2 = (f32[80,1,1,512]{3,2,0,1:T(1,128)S(1)}, f32[80,1,1,512]{3,2,0,1:T(1,128)S(1)}, u32[]{:S(2)}, u32[]{:S(2)}) collective-permute-start(f32[80,1,1,512]{3,2,0,1:T(1,128)S(1)} %get-tuple-element.67), channel_id=1, source_target_pairs={{0,4},{4,8},{8,12},{12,16},{16,20},{20,24},{24,28},{1,5},{5,9},{9,... | collective-permute-start | bytes 491528 | tf_op jit(solution)/shard_map/ppermute | solution.py:18
  28.5 7.3 %collective-permute-start.3 = (f32[80,1,1,512]{3,2,0,1:T(1,128)S(1)}, f32[80,1,1,512]{3,2,0,1:T(1,128)S(1)}, u32[]{:S(2)}, u32[]{:S(2)}) collective-permute-start(f32[80,1,1,512]{3,2,0,1:T(1,128)S(1)} %get-tuple-element.68), channel_id=1, source_target_pairs={{4,0},{8,4},{12,8},{16,12},{20,16},{24,20},{28,24},{5,1},{9,5},{13... | collective-permute-start | bytes 491528 | tf_op jit(solution)/shard_map/ppermute | solution.py:19
  39.7 7.4 %collective-permute-start.4 = (f32[80,1,1,512]{3,2,0,1:T(1,128)S(1)}, f32[80,1,1,512]{3,2,0,1:T(1,128)S(1)}, u32[]{:S(2)}, u32[]{:S(2)}) collective-permute-start(f32[80,1,1,512]{3,2,0,1:T(1,128)S(1)} %get-tuple-element.57), channel_id=1, source_target_pairs={{0,4},{4,8},{8,12},{12,16},{16,20},{20,24},{24,28},{1,5},{5,9},{9,... | collective-permute-start | bytes 491528 | tf_op jit(solution)/shard_map/ppermute | solution.py:18
  44.2 7.7 %collective-permute-start.5 = (f32[80,1,1,512]{3,2,0,1:T(1,128)S(1)}, f32[80,1,1,512]{3,2,0,1:T(1,128)S(1)}, u32[]{:S(2)}, u32[]{:S(2)}) collective-permute-start(f32[80,1,1,512]{3,2,0,1:T(1,128)S(1)} %get-tuple-element.58), channel_id=1, source_target_pairs={{4,0},{8,4},{12,8},{16,12},{20,16},{24,20},{28,24},{5,1},{9,5},{13... | collective-permute-start | bytes 491528 | tf_op jit(solution)/shard_map/ppermute | solution.py:19
  53.0 7.4 %collective-permute-start.6 = (f32[80,1,1,512]{3,2,0,1:T(1,128)S(1)}, f32[80,1,1,512]{3,2,0,1:T(1,128)S(1)}, u32[]{:S(2)}, u32[]{:S(2)}) collective-permute-start(f32[80,1,1,512]{3,2,0,1:T(1,128)S(1)} %get-tuple-element.55), channel_id=1, source_target_pairs={{0,4},{4,8},{8,12},{12,16},{16,20},{20,24},{24,28},{1,5},{5,9},{9,... | collective-permute-start | bytes 491528 | tf_op jit(solution)/shard_map/ppermute | solution.py:18
  57.5 7.9 %collective-permute-start.7 = (f32[80,1,1,512]{3,2,0,1:T(1,128)S(1)}, f32[80,1,1,512]{3,2,0,1:T(1,128)S(1)}, u32[]{:S(2)}, u32[]{:S(2)}) collective-permute-start(f32[80,1,1,512]{3,2,0,1:T(1,128)S(1)} %get-tuple-element.56), channel_id=1, source_target_pairs={{4,0},{8,4},{12,8},{16,12},{20,16},{24,20},{28,24},{5,1},{9,5},{13... | collective-permute-start | bytes 491528 | tf_op jit(solution)/shard_map/ppermute | solution.py:19
  70.1 7.4 %collective-permute-start.8 = (f32[80,1,1,512]{3,2,0,1:T(1,128)S(1)}, f32[80,1,1,512]{3,2,0,1:T(1,128)S(1)}, u32[]{:S(2)}, u32[]{:S(2)}) collective-permute-start(f32[80,1,1,512]{3,2,0,1:T(1,128)S(1)} %get-tuple-element.45), channel_id=1, source_target_pairs={{0,4},{4,8},{8,12},{12,16},{16,20},{20,24},{24,28},{1,5},{5,9},{9,... | collective-permute-start | bytes 491528 | tf_op jit(solution)/shard_map/ppermute | solution.py:18
  74.7 7.9 %collective-permute-start.9 = (f32[80,1,1,512]{3,2,0,1:T(1,128)S(1)}, f32[80,1,1,512]{3,2,0,1:T(1,128)S(1)}, u32[]{:S(2)}, u32[]{:S(2)}) collective-permute-start(f32[80,1,1,512]{3,2,0,1:T(1,128)S(1)} %get-tuple-element.46), channel_id=1, source_target_pairs={{4,0},{8,4},{12,8},{16,12},{20,16},{24,20},{28,24},{5,1},{9,5},{13... | collective-permute-start | bytes 491528 | tf_op jit(solution)/shard_map/ppermute | solution.py:19
  83.5 7.4 %collective-permute-start.10 = (f32[80,1,1,512]{3,2,0,1:T(1,128)S(1)}, f32[80,1,1,512]{3,2,0,1:T(1,128)S(1)}, u32[]{:S(2)}, u32[]{:S(2)}) collective-permute-start(f32[80,1,1,512]{3,2,0,1:T(1,128)S(1)} %get-tuple-element.43), channel_id=1, source_target_pairs={{0,4},{4,8},{8,12},{12,16},{16,20},{20,24},{24,28},{1,5},{5,9},{9,... | collective-permute-start | bytes 491528 | tf_op jit(solution)/shard_map/ppermute | solution.py:18
  88.1 7.9 %collective-permute-start.11 = (f32[80,1,1,512]{3,2,0,1:T(1,128)S(1)}, f32[80,1,1,512]{3,2,0,1:T(1,128)S(1)}, u32[]{:S(2)}, u32[]{:S(2)}) collective-permute-start(f32[80,1,1,512]{3,2,0,1:T(1,128)S(1)} %get-tuple-element.44), channel_id=1, source_target_pairs={{4,0},{8,4},{12,8},{16,12},{20,16},{24,20},{28,24},{5,1},{9,5},{13... | collective-permute-start | bytes 491528 | tf_op jit(solution)/shard_map/ppermute | solution.py:19
  187.2 10.6 %collective-permute-start.12 = (f32[80,1,1,512]{3,2,0,1:T(1,128)S(1)}, f32[80,1,1,512]{3,2,0,1:T(1,128)S(1)}, u32[]{:S(2)}, u32[]{:S(2)}) collective-permute-start(f32[80,1,1,512]{3,2,0,1:T(1,128)S(1)} %get-tuple-element.33), channel_id=1, source_target_pairs={{0,4},{4,8},{8,12},{12,16},{16,20},{20,24},{24,28},{1,5},{5,9},{9,... | collective-permute-start | bytes 491528 | tf_op jit(solution)/shard_map/ppermute | solution.py:18
  191.4 7.2 %collective-permute-start.13 = (f32[80,1,1,512]{3,2,0,1:T(1,128)S(1)}, f32[80,1,1,512]{3,2,0,1:T(1,128)S(1)}, u32[]{:S(2)}, u32[]{:S(2)}) collective-permute-start(f32[80,1,1,512]{3,2,0,1:T(1,128)S(1)} %get-tuple-element.34), channel_id=1, source_target_pairs={{4,0},{8,4},{12,8},{16,12},{20,16},{24,20},{28,24},{5,1},{9,5},{13... | collective-permute-start | bytes 491528 | tf_op jit(solution)/shard_map/ppermute | solution.py:19
  199.6 6.4 %collective-permute-start.14 = (f32[80,1,1,512]{3,2,0,1:T(1,128)S(1)}, f32[80,1,1,512]{3,2,0,1:T(1,128)S(1)}, u32[]{:S(2)}, u32[]{:S(2)}) collective-permute-start(f32[80,1,1,512]{3,2,0,1:T(1,128)S(1)} %get-tuple-element.31), channel_id=1, source_target_pairs={{0,4},{4,8},{8,12},{12,16},{16,20},{20,24},{24,28},{1,5},{5,9},{9,... | collective-permute-start | bytes 491528 | tf_op jit(solution)/shard_map/ppermute | solution.py:18
  203.1 7.2 %collective-permute-start.15 = (f32[80,1,1,512]{3,2,0,1:T(1,128)S(1)}, f32[80,1,1,512]{3,2,0,1:T(1,128)S(1)}, u32[]{:S(2)}, u32[]{:S(2)}) collective-permute-start(f32[80,1,1,512]{3,2,0,1:T(1,128)S(1)} %get-tuple-element.32), channel_id=1, source_target_pairs={{4,0},{8,4},{12,8},{16,12},{20,16},{24,20},{28,24},{5,1},{9,5},{13... | collective-permute-start | bytes 491528 | tf_op jit(solution)/shard_map/ppermute | solution.py:19
  215.0 6.5 %collective-permute-start.16 = (f32[80,1,1,512]{3,2,0,1:T(1,128)S(1)}, f32[80,1,1,512]{3,2,0,1:T(1,128)S(1)}, u32[]{:S(2)}, u32[]{:S(2)}) collective-permute-start(f32[80,1,1,512]{3,2,0,1:T(1,128)S(1)} %get-tuple-element.21), channel_id=1, source_target_pairs={{0,4},{4,8},{8,12},{12,16},{16,20},{20,24},{24,28},{1,5},{5,9},{9,... | collective-permute-start | bytes 491528 | tf_op jit(solution)/shard_map/ppermute | solution.py:18
  218.8 7.2 %collective-permute-start.17 = (f32[80,1,1,512]{3,2,0,1:T(1,128)S(1)}, f32[80,1,1,512]{3,2,0,1:T(1,128)S(1)}, u32[]{:S(2)}, u32[]{:S(2)}) collective-permute-start(f32[80,1,1,512]{3,2,0,1:T(1,128)S(1)} %get-tuple-element.22), channel_id=1, source_target_pairs={{4,0},{8,4},{12,8},{16,12},{20,16},{24,20},{28,24},{5,1},{9,5},{13... | collective-permute-start | bytes 491528 | tf_op jit(solution)/shard_map/ppermute | solution.py:19
  227.0 7.2 %collective-permute-start.18 = (f32[80,1,1,512]{3,2,0,1:T(1,128)S(1)}, f32[80,1,1,512]{3,2,0,1:T(1,128)S(1)}, u32[]{:S(2)}, u32[]{:S(2)}) collective-permute-start(f32[80,1,1,512]{3,2,0,1:T(1,128)S(1)} %get-tuple-element.19), channel_id=1, source_target_pairs={{0,4},{4,8},{8,12},{12,16},{16,20},{20,24},{24,28},{1,5},{5,9},{9,... | collective-permute-start | bytes 491528 | tf_op jit(solution)/shard_map/ppermute | solution.py:18
  231.4 7.9 %collective-permute-start.19 = (f32[80,1,1,512]{3,2,0,1:T(1,128)S(1)}, f32[80,1,1,512]{3,2,0,1:T(1,128)S(1)}, u32[]{:S(2)}, u32[]{:S(2)}) collective-permute-start(f32[80,1,1,512]{3,2,0,1:T(1,128)S(1)} %get-tuple-element.20), channel_id=1, source_target_pairs={{4,0},{8,4},{12,8},{16,12},{20,16},{24,20},{28,24},{5,1},{9,5},{13... | collective-permute-start | bytes 491528 | tf_op jit(solution)/shard_map/ppermute | solution.py:19
  287.1 6.0 %copy-start = (bf16[20,4,2,512]{3,2,1,0:T(2,128)(2,1)S(1)}, bf16[20,4,2,512]{3,2,1,0:T(2,128)(2,1)}, u32[]{:S(2)}) copy-start(bf16[20,4,2,512]{3,2,1,0:T(2,128)(2,1)} %param.4) | copy-start | bytes 491524
  287.4 5.7 %copy-start.2 = (f32[2,512]{1,0:T(2,128)}, f32[2,512]{1,0:T(2,128)S(1)}, u32[]{:S(2)}) copy-start(f32[2,512]{1,0:T(2,128)S(1)} %multiply_reduce_fusion) | copy-start | bytes 12292
where the time goes:
time: 295 us; the launch traced here: 294 us
  blocking collectives  131 us (44%)
  waiting for transfers between devices  64.3 us (22%)
  starting transfers between devices  59.9 us (20%)
  other arithmetic  23 us (8%)
  local copies, waits for them, and re-layouts  11.1 us (4%)
  between operations  5.15 us (2%)
    psum x2, blocking collectives, norm_of(): return lax.psum(jnp.sum(residual * residual), ('grid', 'mem'))  82.7 us
    ppermute x10, waiting for transfers between devices, padded(): after = lax.ppermute(leading, axis, down)  43.5 us
    ppermute x10, starting transfers between devices, padded(): before = lax.ppermute(last, axis, up)  42.3 us
    psum x1, blocking collectives, local(): step_size = norm_now / lax.psum(jnp.sum(direction * image), ('grid', 'mem'))  42.2 us
    ppermute x10, waiting for transfers between devices, padded(): before = lax.ppermute(last, axis, up)  18.5 us
    ppermute x10, starting transfers between devices, padded(): after = lax.ppermute(leading, axis, down)  13.3 us
    add x10, other arithmetic, smooth(): centre + diffusion * (extended[:, :, :-2] + extended[:, :, 2:] - 2.0 * ce...  7.27 us
    add x6, other arithmetic, smooth(): field + diffusion * (jnp.roll(field, 1, 3) + jnp.roll(field, -1, 3) - 2.0...  6.6 us
  transfers between devices with their start and end apart: 21, of which 21 were waited for; matrix products, arithmetic and copies ran while one was open for 1% of the time, Pallas kernels for 0%

commit v1 on v0

--- a/solution.py
+++ b/solution.py
@@ -43,7 +43,21 @@
 def local(members, innovation, observed_count, obs_precision):
     mem_index = lax.axis_index("mem")
     level_share = members.shape[1] // lax.axis_size("mem")
-    perturbed = lax.all_to_all(members, "mem", split_axis=1, concat_axis=0, tiled=True)
+    next_value = jax.lax.axis_index("mem")
+    shaped = jax.lax.axis_size("mem")
+    later, tall = (shaped, next_value)
+    base_arr = list(members.shape)
+    frame_out = members.shape[1] // later
+    base_arr[1] = frame_out
+    w2 = base_arr[0]
+    base_arr[0] = w2 * later
+    perturbed = jnp.zeros(base_arr, members.dtype)
+    for num in range(later):
+        w1 = lax.dynamic_slice_in_dim(members, (tall ^ num) * frame_out, frame_out, axis=1)
+        if num:
+            block_now = tuple(((kk, kk ^ num) for kk in range(later)))
+            w1 = jax.lax.ppermute(w1, "mem", block_now)
+        perturbed = lax.dynamic_update_slice_in_dim(perturbed, w1, (tall ^ num) * w2, axis=0)
     precision = lax.dynamic_slice_in_dim(obs_precision, mem_index * level_share, level_share, 0)
     local_innovation = lax.dynamic_slice_in_dim(innovation, mem_index * level_share, level_share, 0)
     weight = observed_count.astype(jnp.float32)[None] * precision[:, None, None]

time: 295 us -> 292 us (0.990)
    all_to_all x1 -> x0, starting transfers between devices: 4.26 us -> none  [local(): lax.all_to_all(members, 'mem', split_axis=1, concat_axis=0, tiled=True)]
    ppermute x0 -> x3, starting transfers between devices: none -> 3.22 us  [local(): w1 = jax.lax.ppermute(w1, 'mem', block_now)]
  transfers between devices with their start and end apart: 21 -> 23, of which waited for: 21 -> 21; matrix products, arithmetic and copies ran while one was open for 1% -> 1% of each run, Pallas kernels for 0% -> 0%
where the time goes in v1:
time: 292 us; the launch traced here: 291 us
  blocking collectives  131 us (45%)
  waiting for transfers between devices  63.3 us (22%)
  starting transfers between devices  58.1 us (20%)
  other arithmetic  23.3 us (8%)
  local copies, waits for them, and re-layouts  9.84 us (3%)
  between operations  5.07 us (2%)
    psum x2, blocking collectives, norm_of(): return lax.psum(jnp.sum(residual * residual), ('grid', 'mem'))  83.5 us
    ppermute x10, waiting for transfers between devices, padded(): after = lax.ppermute(leading, axis, down)  43 us
    psum x1, blocking collectives, local(): step_size = norm_now / lax.psum(jnp.sum(direction * image), ('grid', 'mem'))  42.2 us
    ppermute x10, starting transfers between devices, padded(): before = lax.ppermute(last, axis, up)  41.6 us
    ppermute x10, waiting for transfers between devices, padded(): before = lax.ppermute(last, axis, up)  18.3 us
    ppermute x10, starting transfers between devices, padded(): after = lax.ppermute(leading, axis, down)  13.3 us
    add x10, other arithmetic, smooth(): centre + diffusion * (extended[:, :, :-2] + extended[:, :, 2:] - 2.0 * ce...  7.28 us
    add x6, other arithmetic, smooth(): field + diffusion * (jnp.roll(field, 1, 3) + jnp.roll(field, -1, 3) - 2.0...  6.59 us
  transfers between devices with their start and end apart: 23, of which 21 were waited for; matrix products, arithmetic and copies ran while one was open for 1% of the time, Pallas kernels for 0%

profile of v1, /device:TPU:0, one launch (start us, length us, event | category | flops | bytes accessed | tf_op | source)
XLA Modules:
  0.0 291.0 jit_solution(3940848991839391804)
XLA Ops:
  1.7 2.5 collective-permute-start.2
  6.9 2.0 collective-permute-done.1
  9.4 3.4 %collective-permute-start.3 = (f32[80,1,1,512]{3,2,1,0:T(1,128)S(1)}, f32[80,1,1,512]{3,2,1,0:T(1,128)S(1)}, u32[]{:S(2)}, u32[]{:S(2)}) collective-permute-start(f32[80,1,1,512]{3,2,1,0:T(1,128)S(1)} %get-tuple-element.69), channel_id=1, source_target_pairs={{0,4},{4,8},{8,12},{12,16},{16,20},{20,24},{24,28},{1,5},{5,9},{9,... | collective-permute-start | bytes 491528 | tf_op jit(solution)/shard_map/ppermute | solution.py:18
  14.1 1.5 collective-permute-done.3
  15.6 4.4 %collective-permute-done.4 = f32[80,1,1,512]{3,2,1,0:T(1,128)S(1)} collective-permute-done((f32[80,1,1,512]{3,2,1,0:T(1,128)S(1)}, f32[80,1,1,512]{3,2,1,0:T(1,128)S(1)}, u32[]{:S(2)}, u32[]{:S(2)}) %collective-permute-start.4) | collective-permute-done | bytes 163872 | tf_op jit(solution)/shard_map/ppermute | solution.py:19
  21.0 4.4 %collective-permute-start.5 = (f32[80,1,1,512]{3,2,1,0:T(1,128)S(1)}, f32[80,1,1,512]{3,2,1,0:T(1,128)S(1)}, u32[]{:S(2)}, u32[]{:S(2)}) collective-permute-start(f32[80,1,1,512]{3,2,1,0:T(1,128)S(1)} %get-tuple-element.67), channel_id=1, source_target_pairs={{0,4},{4,8},{8,12},{12,16},{16,20},{20,24},{24,28},{1,5},{5,9},{9,... | collective-permute-start | bytes 491528 | tf_op jit(solution)/shard_map/ppermute | solution.py:18
  26.6 1.5 collective-permute-done.5
  28.1 4.4 %collective-permute-done.6 = f32[80,1,1,512]{3,2,1,0:T(1,128)S(1)} collective-permute-done((f32[80,1,1,512]{3,2,1,0:T(1,128)S(1)}, f32[80,1,1,512]{3,2,1,0:T(1,128)S(1)}, u32[]{:S(2)}, u32[]{:S(2)}) %collective-permute-start.6) | collective-permute-done | bytes 163872 | tf_op jit(solution)/shard_map/ppermute | solution.py:19
  36.5 4.4 %collective-permute-start.7 = (f32[80,1,1,512]{3,2,1,0:T(1,128)S(1)}, f32[80,1,1,512]{3,2,1,0:T(1,128)S(1)}, u32[]{:S(2)}, u32[]{:S(2)}) collective-permute-start(f32[80,1,1,512]{3,2,1,0:T(1,128)S(1)} %get-tuple-element.57), channel_id=1, source_target_pairs={{0,4},{4,8},{8,12},{12,16},{16,20},{20,24},{24,28},{1,5},{5,9},{9,... | collective-permute-start | bytes 491528 | tf_op jit(solution)/shard_map/ppermute | solution.py:18
  42.2 1.5 collective-permute-done.7
  43.7 4.5 %collective-permute-done.8 = f32[80,1,1,512]{3,2,1,0:T(1,128)S(1)} collective-permute-done((f32[80,1,1,512]{3,2,1,0:T(1,128)S(1)}, f32[80,1,1,512]{3,2,1,0:T(1,128)S(1)}, u32[]{:S(2)}, u32[]{:S(2)}) %collective-permute-start.8) | collective-permute-done | bytes 163872 | tf_op jit(solution)/shard_map/ppermute | solution.py:19
  49.2 4.5 %collective-permute-start.9 = (f32[80,1,1,512]{3,2,1,0:T(1,128)S(1)}, f32[80,1,1,512]{3,2,1,0:T(1,128)S(1)}, u32[]{:S(2)}, u32[]{:S(2)}) collective-permute-start(f32[80,1,1,512]{3,2,1,0:T(1,128)S(1)} %get-tuple-element.55), channel_id=1, source_target_pairs={{0,4},{4,8},{8,12},{12,16},{16,20},{20,24},{24,28},{1,5},{5,9},{9,... | collective-permute-start | bytes 491528 | tf_op jit(solution)/shard_map/ppermute | solution.py:18
  55.0 1.5 collective-permute-done.9
  56.5 4.9 %collective-permute-done.10 = f32[80,1,1,512]{3,2,1,0:T(1,128)S(1)} collective-permute-done((f32[80,1,1,512]{3,2,1,0:T(1,128)S(1)}, f32[80,1,1,512]{3,2,1,0:T(1,128)S(1)}, u32[]{:S(2)}, u32[]{:S(2)}) %collective-permute-start.10) | collective-permute-done | bytes 163872 | tf_op jit(solution)/shard_map/ppermute | solution.py:19
  66.3 4.5 %collective-permute-start.11 = (f32[80,1,1,512]{3,2,1,0:T(1,128)S(1)}, f32[80,1,1,512]{3,2,1,0:T(1,128)S(1)}, u32[]{:S(2)}, u32[]{:S(2)}) collective-permute-start(f32[80,1,1,512]{3,2,1,0:T(1,128)S(1)} %get-tuple-element.45), channel_id=1, source_target_pairs={{0,4},{4,8},{8,12},{12,16},{16,20},{20,24},{24,28},{1,5},{5,9},{9,... | collective-permute-start | bytes 491528 | tf_op jit(solution)/shard_map/ppermute | solution.py:18
  73.6 5.2 %collective-permute-done.12 = f32[80,1,1,512]{3,2,1,0:T(1,128)S(1)} collective-permute-done((f32[80,1,1,512]{3,2,1,0:T(1,128)S(1)}, f32[80,1,1,512]{3,2,1,0:T(1,128)S(1)}, u32[]{:S(2)}, u32[]{:S(2)}) %collective-permute-start.12) | collective-permute-done | bytes 163872 | tf_op jit(solution)/shard_map/ppermute | solution.py:19
  79.9 4.5 %collective-permute-start.13 = (f32[80,1,1,512]{3,2,1,0:T(1,128)S(1)}, f32[80,1,1,512]{3,2,1,0:T(1,128)S(1)}, u32[]{:S(2)}, u32[]{:S(2)}) collective-permute-start(f32[80,1,1,512]{3,2,1,0:T(1,128)S(1)} %get-tuple-element.43), channel_id=1, source_target_pairs={{0,4},{4,8},{8,12},{12,16},{16,20},{20,24},{24,28},{1,5},{5,9},{9,... | collective-permute-start | bytes 491528 | tf_op jit(solution)/shard_map/ppermute | solution.py:18
  85.7 1.5 collective-permute-done.13
  87.2 4.9 %collective-permute-done.14 = f32[80,1,1,512]{3,2,1,0:T(1,128)S(1)} collective-permute-done((f32[80,1,1,512]{3,2,1,0:T(1,128)S(1)}, f32[80,1,1,512]{3,2,1,0:T(1,128)S(1)}, u32[]{:S(2)}, u32[]{:S(2)}) %collective-permute-start.14) | collective-permute-done | bytes 163872 | tf_op jit(solution)/shard_map/ppermute | solution.py:19
  96.6 42.7 %all-reduce = (f32[]{:T(128)}, f32[]{:T(128)}) all-reduce(f32[]{:T(128)} %get-tuple-element.3, f32[]{:T(128)} %get-tuple-element.2), channel_id=1, replica_groups=mesh['grid'=8,'mem'=4] {'grid','mem'}, use_global_device_ids=true, to_apply=%region_1.2 | all-reduce | flops 2 | bytes 16 | tf_op jit(solution)/shard_map/psum | solution.py:40
  141.5 40.8 %psum.30 = f32[]{:T(128)} all-reduce(f32[]{:T(128)} %multiply_reduce_fusion), channel_id=1, replica_groups=mesh['grid'=8,'mem'=4] {'grid','mem'}, use_global_device_ids=true, to_apply=%region_6.7 | all-reduce | flops 1 | bytes 8 | tf_op jit(solution)/shard_map/psum | solution.py:40
  184.1 4.2 %collective-permute-start.15 = (f32[80,1,1,512]{3,2,1,0:T(1,128)S(1)}, f32[80,1,1,512]{3,2,1,0:T(1,128)S(1)}, u32[]{:S(2)}, u32[]{:S(2)}) collective-permute-start(f32[80,1,1,512]{3,2,1,0:T(1,128)S(1)} %get-tuple-element.33), channel_id=1, source_target_pairs={{0,4},{4,8},{8,12},{12,16},{16,20},{20,24},{24,28},{1,5},{5,9},{9,... | collective-permute-start | bytes 491528 | tf_op jit(solution)/shard_map/ppermute | solution.py:18
  189.6 5.1 %collective-permute-done.15 = f32[80,1,1,512]{3,2,1,0:T(1,128)S(1)} collective-permute-done((f32[80,1,1,512]{3,2,1,0:T(1,128)S(1)}, f32[80,1,1,512]{3,2,1,0:T(1,128)S(1)}, u32[]{:S(2)}, u32[]{:S(2)}) %collective-permute-start.15) | collective-permute-done | bytes 163872 | tf_op jit(solution)/shard_map/ppermute | solution.py:18
  196.5 3.5 %collective-permute-start.17 = (f32[80,1,1,512]{3,2,1,0:T(1,128)S(1)}, f32[80,1,1,512]{3,2,1,0:T(1,128)S(1)}, u32[]{:S(2)}, u32[]{:S(2)}) collective-permute-start(f32[80,1,1,512]{3,2,1,0:T(1,128)S(1)} %get-tuple-element.31), channel_id=1, source_target_pairs={{0,4},{4,8},{8,12},{12,16},{16,20},{20,24},{24,28},{1,5},{5,9},{9,... | collective-permute-start | bytes 491528 | tf_op jit(solution)/shard_map/ppermute | solution.py:18
  200.1 1.5 collective-permute-start.18
  202.9 4.4 %collective-permute-done.18 = f32[80,1,1,512]{3,2,1,0:T(1,128)S(1)} collective-permute-done((f32[80,1,1,512]{3,2,1,0:T(1,128)S(1)}, f32[80,1,1,512]{3,2,1,0:T(1,128)S(1)}, u32[]{:S(2)}, u32[]{:S(2)}) %collective-permute-start.18) | collective-permute-done | bytes 163872 | tf_op jit(solution)/shard_map/ppermute | solution.py:19
  212.1 3.7 %collective-permute-start.19 = (f32[80,1,1,512]{3,2,1,0:T(1,128)S(1)}, f32[80,1,1,512]{3,2,1,0:T(1,128)S(1)}, u32[]{:S(2)}, u32[]{:S(2)}) collective-permute-start(f32[80,1,1,512]{3,2,1,0:T(1,128)S(1)} %get-tuple-element.21), channel_id=1, source_target_pairs={{0,4},{4,8},{8,12},{12,16},{16,20},{20,24},{24,28},{1,5},{5,9},{9,... | collective-permute-start | bytes 491528 | tf_op jit(solution)/shard_map/ppermute | solution.py:18
  218.6 4.4 %collective-permute-done.20 = f32[80,1,1,512]{3,2,1,0:T(1,128)S(1)} collective-permute-done((f32[80,1,1,512]{3,2,1,0:T(1,128)S(1)}, f32[80,1,1,512]{3,2,1,0:T(1,128)S(1)}, u32[]{:S(2)}, u32[]{:S(2)}) %collective-permute-start.20) | collective-permute-done | bytes 163872 | tf_op jit(solution)/shard_map/ppermute | solution.py:19
  224.0 4.4 %collective-permute-start.21 = (f32[80,1,1,512]{3,2,1,0:T(1,128)S(1)}, f32[80,1,1,512]{3,2,1,0:T(1,128)S(1)}, u32[]{:S(2)}, u32[]{:S(2)}) collective-permute-start(f32[80,1,1,512]{3,2,1,0:T(1,128)S(1)} %get-tuple-element.19), channel_id=1, source_target_pairs={{0,4},{4,8},{8,12},{12,16},{16,20},{20,24},{24,28},{1,5},{5,9},{9,... | collective-permute-start | bytes 491528 | tf_op jit(solution)/shard_map/ppermute | solution.py:18
  231.2 5.1 %collective-permute-done.22 = f32[80,1,1,512]{3,2,1,0:T(1,128)S(1)} collective-permute-done((f32[80,1,1,512]{3,2,1,0:T(1,128)S(1)}, f32[80,1,1,512]{3,2,1,0:T(1,128)S(1)}, u32[]{:S(2)}, u32[]{:S(2)}) %collective-permute-start.22) | collective-permute-done | bytes 163872 | tf_op jit(solution)/shard_map/ppermute | solution.py:19
  240.7 42.2 %psum.31 = f32[]{:T(128)} all-reduce(f32[]{:T(128)} %fusion), channel_id=1, replica_groups=mesh['grid'=8,'mem'=4] {'grid','mem'}, use_global_device_ids=true, to_apply=%region_9.10 | all-reduce | flops 1 | bytes 8 | tf_op jit(solution)/shard_map/psum | solution.py:74
  284.5 5.7 %all-gather.1 = f32[4,2,512]{2,1,0:T(2,128)S(1)} all-gather(f32[1,2,512]{2,1,0:T(2,128)S(1)} %bitcast.8), channel_id=2, replica_groups=mesh['grid'=8,'mem'=4] {'mem'}, dimensions={0}, use_global_device_ids=true | all-gather | bytes 20480 | tf_op jit(solution)/shard_map/all_gather | solution.py:82
  (92 shorter events, 52.2 us)
Async XLA Ops:
  0.6 0.9 copy-start
  1.5 3.4 %copy-start.3 = (f32[4]{0:T(128)S(1)}, f32[4]{0:T(128)}, u32[]{:S(2)}) copy-start(f32[4]{0:T(128)} %param.7) | copy-start | bytes 52
  1.7 3.8 %copy-start.1 = (s32[2,512]{1,0:T(2,128)S(1)}, s32[2,512]{1,0:T(2,128)}, u32[]{:S(2)}) copy-start(s32[2,512]{1,0:T(2,128)} %param.6) | copy-start | bytes 12292
  1.7 7.2 %collective-permute-start.2 = (bf16[20,1,2,512]{3,2,1,0:T(2,128)(2,1)S(1)}, bf16[20,1,2,512]{3,2,1,0:T(2,128)(2,1)S(1)}, u32[]{:S(2)}, u32[]{:S(2)}) collective-permute-start(bf16[20,1,2,512]{3,2,1,0:T(2,128)(2,1)S(1)} %get-tuple-element.71), channel_id=1, source_target_pairs={{0,3},{1,2},{2,1},{3,0},{4,7},{5,6},{6,5},{7,4},{8,11},{9,10},{10,... | collective-permute-start | bytes 122888 | tf_op jit(solution)/shard_map/ppermute | solution.py:59
  4.2 2.6 collective-permute-start
  4.9 4.0 %collective-permute-start.1 = (bf16[20,1,2,512]{3,2,1,0:T(2,128)(2,1)S(1)}, bf16[20,1,2,512]{3,2,1,0:T(2,128)(2,1)S(1)}, u32[]{:S(2)}, u32[]{:S(2)}) collective-permute-start(bf16[20,1,2,512]{3,2,1,0:T(2,128)(2,1)S(1)} %get-tuple-element.74), channel_id=1, source_target_pairs={{0,2},{1,3},{2,0},{3,1},{4,6},{5,7},{6,4},{7,5},{8,10},{9,11},{10,... | collective-permute-start | bytes 122888 | tf_op jit(solution)/shard_map/ppermute | solution.py:59
  9.4 6.2 %collective-permute-start.3 = (f32[80,1,1,512]{3,2,1,0:T(1,128)S(1)}, f32[80,1,1,512]{3,2,1,0:T(1,128)S(1)}, u32[]{:S(2)}, u32[]{:S(2)}) collective-permute-start(f32[80,1,1,512]{3,2,1,0:T(1,128)S(1)} %get-tuple-element.69), channel_id=1, source_target_pairs={{0,4},{4,8},{8,12},{12,16},{16,20},{20,24},{24,28},{1,5},{5,9},{9,... | collective-permute-start | bytes 491528 | tf_op jit(solution)/shard_map/ppermute | solution.py:18
  12.8 7.2 %collective-permute-start.4 = (f32[80,1,1,512]{3,2,1,0:T(1,128)S(1)}, f32[80,1,1,512]{3,2,1,0:T(1,128)S(1)}, u32[]{:S(2)}, u32[]{:S(2)}) collective-permute-start(f32[80,1,1,512]{3,2,1,0:T(1,128)S(1)} %get-tuple-element.70), channel_id=1, source_target_pairs={{4,0},{8,4},{12,8},{16,12},{20,16},{24,20},{28,24},{5,1},{9,5},{13... | collective-permute-start | bytes 491528 | tf_op jit(solution)/shard_map/ppermute | solution.py:19
  21.0 7.2 %collective-permute-start.5 = (f32[80,1,1,512]{3,2,1,0:T(1,128)S(1)}, f32[80,1,1,512]{3,2,1,0:T(1,128)S(1)}, u32[]{:S(2)}, u32[]{:S(2)}) collective-permute-start(f32[80,1,1,512]{3,2,1,0:T(1,128)S(1)} %get-tuple-element.67), channel_id=1, source_target_pairs={{0,4},{4,8},{8,12},{12,16},{16,20},{20,24},{24,28},{1,5},{5,9},{9,... | collective-permute-start | bytes 491528 | tf_op jit(solution)/shard_map/ppermute | solution.py:18
  25.3 7.2 %collective-permute-start.6 = (f32[80,1,1,512]{3,2,1,0:T(1,128)S(1)}, f32[80,1,1,512]{3,2,1,0:T(1,128)S(1)}, u32[]{:S(2)}, u32[]{:S(2)}) collective-permute-start(f32[80,1,1,512]{3,2,1,0:T(1,128)S(1)} %get-tuple-element.68), channel_id=1, source_target_pairs={{4,0},{8,4},{12,8},{16,12},{20,16},{24,20},{28,24},{5,1},{9,5},{13... | collective-permute-start | bytes 491528 | tf_op jit(solution)/shard_map/ppermute | solution.py:19
  36.5 7.2 %collective-permute-start.7 = (f32[80,1,1,512]{3,2,1,0:T(1,128)S(1)}, f32[80,1,1,512]{3,2,1,0:T(1,128)S(1)}, u32[]{:S(2)}, u32[]{:S(2)}) collective-permute-start(f32[80,1,1,512]{3,2,1,0:T(1,128)S(1)} %get-tuple-element.57), channel_id=1, source_target_pairs={{0,4},{4,8},{8,12},{12,16},{16,20},{20,24},{24,28},{1,5},{5,9},{9,... | collective-permute-start | bytes 491528 | tf_op jit(solution)/shard_map/ppermute | solution.py:18
  40.9 7.3 %collective-permute-start.8 = (f32[80,1,1,512]{3,2,1,0:T(1,128)S(1)}, f32[80,1,1,512]{3,2,1,0:T(1,128)S(1)}, u32[]{:S(2)}, u32[]{:S(2)}) collective-permute-start(f32[80,1,1,512]{3,2,1,0:T(1,128)S(1)} %get-tuple-element.58), channel_id=1, source_target_pairs={{4,0},{8,4},{12,8},{16,12},{20,16},{24,20},{28,24},{5,1},{9,5},{13... | collective-permute-start | bytes 491528 | tf_op jit(solution)/shard_map/ppermute | solution.py:19
  49.2 7.4 %collective-permute-start.9 = (f32[80,1,1,512]{3,2,1,0:T(1,128)S(1)}, f32[80,1,1,512]{3,2,1,0:T(1,128)S(1)}, u32[]{:S(2)}, u32[]{:S(2)}) collective-permute-start(f32[80,1,1,512]{3,2,1,0:T(1,128)S(1)} %get-tuple-element.55), channel_id=1, source_target_pairs={{0,4},{4,8},{8,12},{12,16},{16,20},{20,24},{24,28},{1,5},{5,9},{9,... | collective-permute-start | bytes 491528 | tf_op jit(solution)/shard_map/ppermute | solution.py:18
  53.7 7.7 %collective-permute-start.10 = (f32[80,1,1,512]{3,2,1,0:T(1,128)S(1)}, f32[80,1,1,512]{3,2,1,0:T(1,128)S(1)}, u32[]{:S(2)}, u32[]{:S(2)}) collective-permute-start(f32[80,1,1,512]{3,2,1,0:T(1,128)S(1)} %get-tuple-element.56), channel_id=1, source_target_pairs={{4,0},{8,4},{12,8},{16,12},{20,16},{24,20},{28,24},{5,1},{9,5},{13... | collective-permute-start | bytes 491528 | tf_op jit(solution)/shard_map/ppermute | solution.py:19
  66.3 7.4 %collective-permute-start.11 = (f32[80,1,1,512]{3,2,1,0:T(1,128)S(1)}, f32[80,1,1,512]{3,2,1,0:T(1,128)S(1)}, u32[]{:S(2)}, u32[]{:S(2)}) collective-permute-start(f32[80,1,1,512]{3,2,1,0:T(1,128)S(1)} %get-tuple-element.45), channel_id=1, source_target_pairs={{0,4},{4,8},{8,12},{12,16},{16,20},{20,24},{24,28},{1,5},{5,9},{9,... | collective-permute-start | bytes 491528 | tf_op jit(solution)/shard_map/ppermute | solution.py:18
  70.8 8.1 %collective-permute-start.12 = (f32[80,1,1,512]{3,2,1,0:T(1,128)S(1)}, f32[80,1,1,512]{3,2,1,0:T(1,128)S(1)}, u32[]{:S(2)}, u32[]{:S(2)}) collective-permute-start(f32[80,1,1,512]{3,2,1,0:T(1,128)S(1)} %get-tuple-element.46), channel_id=1, source_target_pairs={{4,0},{8,4},{12,8},{16,12},{20,16},{24,20},{28,24},{5,1},{9,5},{13... | collective-permute-start | bytes 491528 | tf_op jit(solution)/shard_map/ppermute | solution.py:19
  79.9 7.4 %collective-permute-start.13 = (f32[80,1,1,512]{3,2,1,0:T(1,128)S(1)}, f32[80,1,1,512]{3,2,1,0:T(1,128)S(1)}, u32[]{:S(2)}, u32[]{:S(2)}) collective-permute-start(f32[80,1,1,512]{3,2,1,0:T(1,128)S(1)} %get-tuple-element.43), channel_id=1, source_target_pairs={{0,4},{4,8},{8,12},{12,16},{16,20},{20,24},{24,28},{1,5},{5,9},{9,... | collective-permute-start | bytes 491528 | tf_op jit(solution)/shard_map/ppermute | solution.py:18
  84.4 7.7 %collective-permute-start.14 = (f32[80,1,1,512]{3,2,1,0:T(1,128)S(1)}, f32[80,1,1,512]{3,2,1,0:T(1,128)S(1)}, u32[]{:S(2)}, u32[]{:S(2)}) collective-permute-start(f32[80,1,1,512]{3,2,1,0:T(1,128)S(1)} %get-tuple-element.44), channel_id=1, source_target_pairs={{4,0},{8,4},{12,8},{16,12},{20,16},{24,20},{28,24},{5,1},{9,5},{13... | collective-permute-start | bytes 491528 | tf_op jit(solution)/shard_map/ppermute | solution.py:19
  184.1 10.6 %collective-permute-start.15 = (f32[80,1,1,512]{3,2,1,0:T(1,128)S(1)}, f32[80,1,1,512]{3,2,1,0:T(1,128)S(1)}, u32[]{:S(2)}, u32[]{:S(2)}) collective-permute-start(f32[80,1,1,512]{3,2,1,0:T(1,128)S(1)} %get-tuple-element.33), channel_id=1, source_target_pairs={{0,4},{4,8},{8,12},{12,16},{16,20},{20,24},{24,28},{1,5},{5,9},{9,... | collective-permute-start | bytes 491528 | tf_op jit(solution)/shard_map/ppermute | solution.py:18
  188.3 7.2 %collective-permute-start.16 = (f32[80,1,1,512]{3,2,1,0:T(1,128)S(1)}, f32[80,1,1,512]{3,2,1,0:T(1,128)S(1)}, u32[]{:S(2)}, u32[]{:S(2)}) collective-permute-start(f32[80,1,1,512]{3,2,1,0:T(1,128)S(1)} %get-tuple-element.34), channel_id=1, source_target_pairs={{4,0},{8,4},{12,8},{16,12},{20,16},{24,20},{28,24},{5,1},{9,5},{13... | collective-permute-start | bytes 491528 | tf_op jit(solution)/shard_map/ppermute | solution.py:19
  196.5 6.4 %collective-permute-start.17 = (f32[80,1,1,512]{3,2,1,0:T(1,128)S(1)}, f32[80,1,1,512]{3,2,1,0:T(1,128)S(1)}, u32[]{:S(2)}, u32[]{:S(2)}) collective-permute-start(f32[80,1,1,512]{3,2,1,0:T(1,128)S(1)} %get-tuple-element.31), channel_id=1, source_target_pairs={{0,4},{4,8},{8,12},{12,16},{16,20},{20,24},{24,28},{1,5},{5,9},{9,... | collective-permute-start | bytes 491528 | tf_op jit(solution)/shard_map/ppermute | solution.py:18
  200.1 7.2 %collective-permute-start.18 = (f32[80,1,1,512]{3,2,1,0:T(1,128)S(1)}, f32[80,1,1,512]{3,2,1,0:T(1,128)S(1)}, u32[]{:S(2)}, u32[]{:S(2)}) collective-permute-start(f32[80,1,1,512]{3,2,1,0:T(1,128)S(1)} %get-tuple-element.32), channel_id=1, source_target_pairs={{4,0},{8,4},{12,8},{16,12},{20,16},{24,20},{28,24},{5,1},{9,5},{13... | collective-permute-start | bytes 491528 | tf_op jit(solution)/shard_map/ppermute | solution.py:19
  212.1 6.5 %collective-permute-start.19 = (f32[80,1,1,512]{3,2,1,0:T(1,128)S(1)}, f32[80,1,1,512]{3,2,1,0:T(1,128)S(1)}, u32[]{:S(2)}, u32[]{:S(2)}) collective-permute-start(f32[80,1,1,512]{3,2,1,0:T(1,128)S(1)} %get-tuple-element.21), channel_id=1, source_target_pairs={{0,4},{4,8},{8,12},{12,16},{16,20},{20,24},{24,28},{1,5},{5,9},{9,... | collective-permute-start | bytes 491528 | tf_op jit(solution)/shard_map/ppermute | solution.py:18
  215.8 7.2 %collective-permute-start.20 = (f32[80,1,1,512]{3,2,1,0:T(1,128)S(1)}, f32[80,1,1,512]{3,2,1,0:T(1,128)S(1)}, u32[]{:S(2)}, u32[]{:S(2)}) collective-permute-start(f32[80,1,1,512]{3,2,1,0:T(1,128)S(1)} %get-tuple-element.22), channel_id=1, source_target_pairs={{4,0},{8,4},{12,8},{16,12},{20,16},{24,20},{28,24},{5,1},{9,5},{13... | collective-permute-start | bytes 491528 | tf_op jit(solution)/shard_map/ppermute | solution.py:19
  224.0 7.2 %collective-permute-start.21 = (f32[80,1,1,512]{3,2,1,0:T(1,128)S(1)}, f32[80,1,1,512]{3,2,1,0:T(1,128)S(1)}, u32[]{:S(2)}, u32[]{:S(2)}) collective-permute-start(f32[80,1,1,512]{3,2,1,0:T(1,128)S(1)} %get-tuple-element.19), channel_id=1, source_target_pairs={{0,4},{4,8},{8,12},{12,16},{16,20},{20,24},{24,28},{1,5},{5,9},{9,... | collective-permute-start | bytes 491528 | tf_op jit(solution)/shard_map/ppermute | solution.py:18
  228.4 7.9 %collective-permute-start.22 = (f32[80,1,1,512]{3,2,1,0:T(1,128)S(1)}, f32[80,1,1,512]{3,2,1,0:T(1,128)S(1)}, u32[]{:S(2)}, u32[]{:S(2)}) collective-permute-start(f32[80,1,1,512]{3,2,1,0:T(1,128)S(1)} %get-tuple-element.20), channel_id=1, source_target_pairs={{4,0},{8,4},{12,8},{16,12},{20,16},{24,20},{28,24},{5,1},{9,5},{13... | collective-permute-start | bytes 491528 | tf_op jit(solution)/shard_map/ppermute | solution.py:19
  284.5 5.8 %copy-start.2 = (f32[2,512]{1,0:T(2,128)}, f32[2,512]{1,0:T(2,128)S(1)}, u32[]{:S(2)}) copy-start(f32[2,512]{1,0:T(2,128)S(1)} %fusion.3) | copy-start | bytes 12292
